TPU v7x, 128 devices: a whole 4x4x4 slice. The times are simulated.
128 devices in a mesh: mode: 8 (over x, core), member: 16 (over z, y).
Axes of the slice: x: 4, y: 4, z: 4, core: 2. Of those that a mesh axis runs over, the one named last changes fastest.
Arguments:
- ground_accel: bfloat16 [4, 639], replicated, may hold values from -6 to 6
- modal_kernel: bfloat16 [4096, 512], P(('mode', 'member')), may hold values from -0.25 to 0.25
- mode_shapes: bfloat16 [98304, 4096], P('member', 'mode'), may hold values from -0.09375 to 0.09375
- member_owner: int32 [16384, 1], P('member'), may hold values from 0 to 127; in each aligned block of 128 rows (0 to 127, 128 to 255, ...) at most 2 rows name the same one
- member_group: int32 [16384, 1], P('member'), may hold values from 0 to 3
- record_table: int32 [512, 8], P(('mode', 'member')), may hold values from 0 to 3
- case_coef: float32 [8, 6], replicated, may hold values from -1.5 to 1.5
- gravity: float32 [512, 8], P(('mode', 'member')), may hold values from -10 to 10
Outputs:
- demand: float32 [512, 8], P(('mode', 'member'))
Inputs may be any that keep to these rules, and one draw needn't show every extreme that they name: `member_owner`: in each aligned block of 1024 / 8 members no owner is named more than 2 times, a bound that some block reaches.
All inputs are finite; a program needn't handle non-finite values.
Results may differ from a plain program's by a relative error of at most 0.0065.
Values may be sent and summed in bfloat16 or wider, within the bound.
No kernel may reach another device: no remote copies, remote signals or barrier semaphores. Data moves between devices by JAX's collectives and lax.ppermute only.
A program may use at most 64 MiB of HBM per device.

v0:
```python
import jax
import jax.numpy as jnp
from jax import lax
from jax.sharding import PartitionSpec as P


def lagged_table(ground_accel, tap_count):
    record_count, span_len = ground_accel.shape
    step_count = span_len - tap_count + 1
    tiled = jnp.tile(ground_accel, (1, step_count + 1))[:, : step_count * (span_len + 1)]
    windows = tiled.reshape(record_count, step_count, span_len + 1)[:, :, :tap_count]
    return windows.reshape(record_count * step_count, tap_count)


def local(
    ground_accel,
    modal_kernel,
    mode_shapes,
    member_owner,
    member_group,
    record_table,
    case_coef,
    gravity,
):
    tap_count = modal_kernel.shape[1]
    record_count = ground_accel.shape[0]
    comp_count = case_coef.shape[1]
    group_count = gravity.shape[0]
    n_mode = lax.axis_size("mode")
    n_member = lax.axis_size("member")
    lagged = lagged_table(ground_accel, tap_count)
    local_resp = lax.dot_general(
        modal_kernel[:, ::-1], lagged, (((1,), (1,)), ((), ())), preferred_element_type=jnp.float32
    ).astype(jnp.bfloat16)
    modal_resp = lax.all_gather(local_resp, "member", axis=0, tiled=True)
    own_rows = mode_shapes.shape[0] // n_mode
    forces = lax.psum_scatter(
        jnp.dot(mode_shapes, modal_resp, preferred_element_type=jnp.float32).astype(jnp.bfloat16),
        "mode",
        scatter_dimension=0,
        tiled=True,
    ).astype(jnp.float32)
    members_here = own_rows // comp_count
    owner_total = n_mode * n_member
    slot_depth = max(2, 2 * members_here // owner_total)
    packed = forces.reshape(members_here, comp_count * forces.shape[1])
    first_row = lax.axis_index("mode") * members_here
    owner_ids = lax.dynamic_slice_in_dim(member_owner[:, 0], first_row, members_here)
    group_ids = lax.dynamic_slice_in_dim(member_group[:, 0], first_row, members_here)
    position = jnp.arange(members_here)
    earlier = (owner_ids[:, None] == owner_ids[None, :]) & (position[None, :] < position[:, None])
    member_rank = jnp.sum(earlier.astype(jnp.int32), axis=1)
    slot_index = owner_ids * slot_depth + member_rank
    slot_total = owner_total * slot_depth
    placement = jnp.arange(slot_total)[:, None] == slot_index[None, :]
    outgoing = jnp.dot(placement.astype(jnp.float32), packed, precision=lax.Precision.HIGHEST)
    slot_labels = jnp.max(jnp.where(placement, group_ids[None, :], -1), axis=1)
    incoming, slot_tags = (
        lax.all_to_all(
            outgoing.reshape(owner_total, slot_depth, -1).astype(jnp.bfloat16),
            ("mode", "member"),
            split_axis=0,
            concat_axis=0,
            tiled=True,
        ).astype(jnp.float32),
        lax.all_to_all(
            slot_labels.reshape(owner_total, slot_depth),
            ("mode", "member"),
            split_axis=0,
            concat_axis=0,
            tiled=True,
        ),
    )
    selector = (jnp.arange(group_count)[:, None] == slot_tags.reshape(-1)[None, :]).astype(
        jnp.float32
    )
    group_sums = jnp.dot(
        selector, incoming.reshape(selector.shape[1], -1), precision=lax.Precision.HIGHEST
    )
    group_sums = group_sums.reshape(group_count, comp_count, record_count, -1)
    case_mix = jnp.einsum("sc,gcrt->gsrt", case_coef, group_sums, precision=lax.Precision.HIGHEST)
    record_pick = (record_table[:, :, None] == jnp.arange(record_count)[None, None, :]).astype(
        jnp.float32
    )
    selected = jnp.sum(record_pick[:, :, :, None] * case_mix, axis=2)
    combined = gravity[:, :, None] + selected
    return jnp.max(jnp.abs(combined), axis=2)


def solution(mesh):
    placed = (
        P(),
        P(("mode", "member"), None),
        P("member", "mode"),
        P("member", None),
        P("member", None),
        P(("mode", "member"), None),
        P(),
        P(("mode", "member"), None),
    )
    return jax.shard_map(
        local, mesh=mesh, in_specs=placed, out_specs=P(("mode", "member"), None), check_vma=False
    )
```

profile of v0, /device:TPU:1, one launch (start us, length us, event | category | flops | bytes accessed | tf_op | source)
XLA Modules:
  0.0 134.6 jit_solution(4952856009396040289)
XLA Ops:
  6.5 0.0 copy-start
  6.5 0.0 reduce-scatter.2.cloned.1.call-start
  6.5 1.6 %rev.3 = bf16[32,512]{1,0:T(8,128)(2,1)S(1)} reverse(bf16[32,512]{1,0:T(8,128)(2,1)} %param.9), dimensions={1} | reverse | bytes 65536 | tf_op jit(solution)/shard_map/rev | solution.py:33
  8.2 0.7 tile.4
  8.9 0.6 tile.10
  9.6 0.2 slice.8
  9.8 0.1 copy.27
  9.9 0.2 convolution_convert_fusion.2
  10.2 21.2 %all_gather.3 = bf16[512,512]{1,0:T(8,128)(2,1)S(1)} all-gather(bf16[32,512]{1,0:T(8,128)(2,1)S(1)} %convolution_convert_fusion.2), channel_id=1, replica_groups=mesh['mode'=8,'member'=16] {'member'}, dimensions={0}, use_global_device_ids=true | all-gather | bytes 557056 | tf_op jit(solution)/shard_map/all_gather | solution.py:35
  31.4 8.3 %fusion = bf16[6144,512]{0,1:T(8,128)(2,1)} fusion(bf16[512,512]{1,0:T(8,128)(2,1)S(1)} %all_gather.3, bf16[6144,512]{1,0:T(8,128)(2,1)} %param.10), kind=kOutput, calls=%fused_computation.1 | convolution fusion | flops 3224371200 | bytes 13107200 | tf_op jit(solution)/shard_map/dot_general | solution.py:38
  39.6 0.0 reduce-scatter.2.cloned.1.call-update
  39.7 0.7 dynamic-slice_bitcast_fusion.1
  40.3 0.7 dynamic-slice_bitcast_fusion
  41.0 0.2 convert_reduce_fusion
  41.2 0.7 multiply_add_fusion.1
  41.8 0.1 select_reduce_fusion
  41.9 0.8 all_to_all.9
  42.7 12.8 %all-to-all-start = ((s32[128,1,2]{2,1,0:T(1,128)}), s32[128,1,2]{2,1,0:T(1,128)S(1)}, u32[]{:S(2)}, u32[]{:S(2)}) async-start(s32[128,1,2]{2,1,0:T(1,128)} %bitcast.2), calls=%async_computation | async-start | bytes 131072 | tf_op jit(solution)/shard_map/all_to_all | solution.py:66
  55.5 31.4 %reduce-scatter.2.cloned.1.call-done = bf16[768,512]{0,1:T(8,128)(2,1)} async-done(((bf16[6144,512]{0,1:T(8,128)(2,1)}), bf16[768,512]{0,1:T(8,128)(2,1)}) %reduce-scatter.2.cloned.1.call-update) | async-done | bytes 786448 | tf_op jit(solution)/shard_map/reduce_scatter | solution.py:37
  86.9 1.4 %copy.17 = bf16[768,512]{1,0:T(8,128)(2,1)S(1)} copy(bf16[768,512]{0,1:T(8,128)(2,1)} %reduce-scatter.2.cloned.1.call-done) | data formatting | bytes 1572864 | tf_op jit(solution)/shard_map/reduce_scatter | solution.py:37
  88.3 0.7 reshape.68
  89.0 0.6 convolution_convert_fusion.1
  89.6 2.8 %copy.18 = bf16[128,2,3072]{2,1,0:T(2,128)(2,1)} copy(bf16[128,2,3072]{2,0,1:T(8,128)(2,1)S(1)} %convolution_convert_fusion.1) | data formatting | bytes 3145728 | tf_op jit(solution)/shard_map/convert_element_type | solution.py:60
  92.4 0.0 copy-start.1
  92.4 0.0 all-to-all-done
  92.4 8.5 %all-to-all-start.1 = ((bf16[128,2,3072]{2,1,0:T(2,128)(2,1)}), bf16[128,2,3072]{2,1,0:T(2,128)(2,1)S(1)}, u32[]{:S(2)}, u32[]{:S(2)}) async-start(bf16[128,2,3072]{2,1,0:T(2,128)(2,1)} %copy.18), calls=%async_computation.2 | async-start | bytes 3145728 | tf_op jit(solution)/shard_map/all_to_all | solution.py:59
  100.9 0.0 copy-done.1
  100.9 0.5 broadcast.35
  101.4 0.8 reduce.3
  102.2 0.1 eq.85
  102.4 22.6 %all-to-all-done.1 = bf16[128,2,3072]{2,1,0:T(2,128)(2,1)S(1)} async-done(((bf16[128,2,3072]{2,1,0:T(2,128)(2,1)}), bf16[128,2,3072]{2,1,0:T(2,128)(2,1)S(1)}, u32[]{:S(2)}, u32[]{:S(2)}) %all-to-all-start.1) | async-done | bytes 1572896 | tf_op jit(solution)/shard_map/all_to_all | solution.py:59
  125.0 0.6 reshape.67
  125.6 0.7 copy.19
  126.3 0.0 copy-start.2
  126.3 0.5 fusion.11
  126.8 0.0 copy-done
  126.8 0.2 fusion.2
  127.0 0.0 copy-done.2
  127.0 0.7 abs_reduce_fusion
  (3 shorter events, 0.0 us)
Async XLA Ops:
  6.5 120.3 %copy-start = (f32[8,6]{1,0:T(8,128)S(1)}, f32[8,6]{1,0:T(8,128)}, u32[]{:S(2)}) copy-start(f32[8,6]{1,0:T(8,128)} %param.14) | copy-start | bytes 580
  6.5 80.3 %reduce-scatter.2.cloned.1.call-start = ((), (), s32[]{:S(2)}) async-start(), calls=%async_computation.3 | async-start | bytes 7077888 | tf_op jit(solution)/shard_map/reduce_scatter | solution.py:37
  42.7 49.7 %all-to-all-start = ((s32[128,1,2]{2,1,0:T(1,128)}), s32[128,1,2]{2,1,0:T(1,128)S(1)}, u32[]{:S(2)}, u32[]{:S(2)}) async-start(s32[128,1,2]{2,1,0:T(1,128)} %bitcast.2), calls=%async_computation | async-start | bytes 131072 | tf_op jit(solution)/shard_map/all_to_all | solution.py:66
  92.4 8.5 %copy-start.1 = (s32[4,8]{1,0:T(4,128)S(1)}, s32[4,8]{1,0:T(4,128)}, u32[]{:S(2)}) copy-start(s32[4,8]{1,0:T(4,128)} %param.13) | copy-start | bytes 388
  92.4 32.6 %all-to-all-start.1 = ((bf16[128,2,3072]{2,1,0:T(2,128)(2,1)}), bf16[128,2,3072]{2,1,0:T(2,128)(2,1)S(1)}, u32[]{:S(2)}, u32[]{:S(2)}) async-start(bf16[128,2,3072]{2,1,0:T(2,128)(2,1)} %copy.18), calls=%async_computation.2 | async-start | bytes 3145728 | tf_op jit(solution)/shard_map/all_to_all | solution.py:59
  126.3 0.7 copy-start.2
Sparse Core Ops, SparseCore 0:
  39.8 47.0 reduce-scatter.1
where the time goes:
time: 135 us
  waiting for transfers between devices  54 us (40%)
  starting transfers between devices  21.3 us (16%)
  blocking collectives  21.2 us (16%)
  between operations  13.5 us (10%)
  local copies, waits for them, and re-layouts  12.3 us (9%)
  matrix products  9.84 us (7%)
  other arithmetic  2.5 us (2%)
    reduce_scatter x1, waiting for transfers between devices, local(): lax.psum_scatter(jnp.dot(mode_shapes, modal_resp, preferred_element_type=...  31.4 us
    all_to_all x1, waiting for transfers between devices, local(): lax.all_to_all(outgoing.reshape(owner_total, slot_depth, -1).astype(jnp.b...  22.6 us
    all_gather x1, blocking collectives, local(): modal_resp = lax.all_gather(local_resp, 'member', axis=0, tiled=True)  21.2 us
    all_to_all x1, starting transfers between devices, local(): lax.all_to_all(slot_labels.reshape(owner_total, slot_depth), ('mode', 'me...  12.8 us
    all_to_all x1, starting transfers between devices, local(): lax.all_to_all(outgoing.reshape(owner_total, slot_depth, -1).astype(jnp.b...  8.52 us
    dot_general x1, matrix products, local(): jnp.dot(mode_shapes, modal_resp, preferred_element_type=jnp.float32)  8.28 us
    convert_element_type x1, local copies, waits for them, and re-layouts, local(): outgoing.reshape(owner_total, slot_depth, -1).astype(jnp.bfloat16)  2.77 us
  transfers between devices with their start and end apart: 3, of which 2 were waited for; matrix products, arithmetic and copies ran while one was open for 7% of the time, Pallas kernels for 0%

commit v1 on v0

--- a/solution.py
+++ b/solution.py
@@ -32,7 +32,8 @@
     local_resp = lax.dot_general(
         modal_kernel[:, ::-1], lagged, (((1,), (1,)), ((), ())), preferred_element_type=jnp.float32
     ).astype(jnp.bfloat16)
-    modal_resp = lax.all_gather(local_resp, "member", axis=0, tiled=True)
+    left_arr = lax.all_to_all(jnp.stack(lax.axis_size("member") * [local_resp]), "member", 0, 0)
+    modal_resp = jnp.concatenate(left_arr, axis=0)
     own_rows = mode_shapes.shape[0] // n_mode
     forces = lax.psum_scatter(
         jnp.dot(mode_shapes, modal_resp, preferred_element_type=jnp.float32).astype(jnp.bfloat16),

time: 135 us -> 127 us (0.941)
  starting transfers between devices: 21.3 us -> 15.6 us
  blocking collectives: 21.2 us -> 18.9 us
    all_gather x1 -> x0, blocking collectives: 21.2 us -> none  [local(): modal_resp = lax.all_gather(local_resp, 'member', axis=0, tiled=True)]
    all_to_all x0 -> x1, blocking collectives: none -> 18.9 us  [local(): lax.all_to_all(jnp.stack(lax.axis_size('member') * [local_resp]), 'member...]
    all_to_all x1, starting transfers between devices: 12.8 us -> 7.07 us  [local(): lax.all_to_all(slot_labels.reshape(owner_total, slot_depth), ('mode', 'me...]
where the time goes in v1:
time: 127 us
  waiting for transfers between devices  54 us (43%)
  blocking collectives  18.9 us (15%)
  starting transfers between devices  15.6 us (12%)
  between operations  13.6 us (11%)
  local copies, waits for them, and re-layouts  12.3 us (10%)
  matrix products  9.83 us (8%)
  other arithmetic  2.5 us (2%)
    reduce_scatter x1, waiting for transfers between devices, local(): lax.psum_scatter(jnp.dot(mode_shapes, modal_resp, preferred_element_type=...  31.4 us
    all_to_all x1, waiting for transfers between devices, local(): lax.all_to_all(outgoing.reshape(owner_total, slot_depth, -1).astype(jnp.b...  22.6 us
    all_to_all x1, blocking collectives, local(): lax.all_to_all(jnp.stack(lax.axis_size('member') * [local_resp]), 'member...  18.9 us
    all_to_all x1, starting transfers between devices, local(): lax.all_to_all(outgoing.reshape(owner_total, slot_depth, -1).astype(jnp.b...  8.51 us
    dot_general x1, matrix products, local(): jnp.dot(mode_shapes, modal_resp, preferred_element_type=jnp.float32)  8.27 us
    all_to_all x1, starting transfers between devices, local(): lax.all_to_all(slot_labels.reshape(owner_total, slot_depth), ('mode', 'me...  7.07 us
    convert_element_type x1, local copies, waits for them, and re-layouts, local(): outgoing.reshape(owner_total, slot_depth, -1).astype(jnp.bfloat16)  2.77 us
  transfers between devices with their start and end apart: 3, of which 2 were waited for; matrix products, arithmetic and copies ran while one was open for 7% of the time, Pallas kernels for 0%

profile of v1, /device:TPU:1, one launch (start us, length us, event | category | flops | bytes accessed | tf_op | source)
XLA Modules:
  0.0 126.7 jit_solution(8161426989656635601)
XLA Ops:
  6.5 0.0 copy-start
  6.5 0.0 reduce-scatter.2.cloned.1.call-start
  6.5 1.6 %rev.3 = bf16[32,512]{1,0:T(8,128)(2,1)S(1)} reverse(bf16[32,512]{1,0:T(8,128)(2,1)} %param.9), dimensions={1} | reverse | bytes 65536 | tf_op jit(solution)/shard_map/rev | solution.py:33
  8.2 0.7 tile.4
  8.9 0.6 tile.10
  9.6 0.2 slice.8
  9.8 0.1 copy.27
  9.9 0.2 convolution_convert_fusion.2
  10.2 0.1 stack.2
  10.3 18.9 %all_to_all.19 = bf16[16,32,512]{2,1,0:T(8,128)(2,1)S(1)} all-to-all(bf16[16,32,512]{2,1,0:T(8,128)(2,1)S(1)} %stack.2), channel_id=1, replica_groups=mesh['mode'=8,'member'=16] {'member'}, dimensions={0} | all-to-all | bytes 1048576 | tf_op jit(solution)/shard_map/all_to_all | solution.py:35
  29.2 8.3 %fusion = bf16[6144,512]{0,1:T(8,128)(2,1)} fusion(bf16[512,512]{1,0:T(8,128)(2,1)S(1)} %bitcast.44, bf16[6144,512]{1,0:T(8,128)(2,1)} %param.10), kind=kOutput, calls=%fused_computation.1 | convolution fusion | flops 3224371200 | bytes 13107200 | tf_op jit(solution)/shard_map/dot_general | solution.py:39
  37.4 0.0 reduce-scatter.2.cloned.1.call-update
  37.5 0.7 dynamic-slice_bitcast_fusion.1
  38.1 0.7 dynamic-slice_bitcast_fusion
  38.8 0.2 convert_reduce_fusion
  39.0 0.7 multiply_add_fusion.1
  39.6 0.1 select_reduce_fusion
  39.7 0.8 all_to_all.12
  40.5 7.1 %all-to-all-start = ((s32[128,1,2]{2,1,0:T(1,128)}), s32[128,1,2]{2,1,0:T(1,128)S(1)}, u32[]{:S(2)}, u32[]{:S(2)}) async-start(s32[128,1,2]{2,1,0:T(1,128)} %bitcast.2), calls=%async_computation | async-start | bytes 131072 | tf_op jit(solution)/shard_map/all_to_all | solution.py:67
  47.6 31.4 %reduce-scatter.2.cloned.1.call-done = bf16[768,512]{0,1:T(8,128)(2,1)} async-done(((bf16[6144,512]{0,1:T(8,128)(2,1)}), bf16[768,512]{0,1:T(8,128)(2,1)}) %reduce-scatter.2.cloned.1.call-update) | async-done | bytes 786448 | tf_op jit(solution)/shard_map/reduce_scatter | solution.py:38
  79.0 1.4 %copy.17 = bf16[768,512]{1,0:T(8,128)(2,1)S(1)} copy(bf16[768,512]{0,1:T(8,128)(2,1)} %reduce-scatter.2.cloned.1.call-done) | data formatting | bytes 1572864 | tf_op jit(solution)/shard_map/reduce_scatter | solution.py:38
  80.4 0.7 reshape.74
  81.1 0.6 convolution_convert_fusion.1
  81.7 2.8 %copy.18 = bf16[128,2,3072]{2,1,0:T(2,128)(2,1)} copy(bf16[128,2,3072]{2,0,1:T(8,128)(2,1)S(1)} %convolution_convert_fusion.1) | data formatting | bytes 3145728 | tf_op jit(solution)/shard_map/convert_element_type | solution.py:61
  84.5 0.0 copy-start.1
  84.5 0.0 all-to-all-done
  84.5 8.5 %all-to-all-start.2 = ((bf16[128,2,3072]{2,1,0:T(2,128)(2,1)}), bf16[128,2,3072]{2,1,0:T(2,128)(2,1)S(1)}, u32[]{:S(2)}, u32[]{:S(2)}) async-start(bf16[128,2,3072]{2,1,0:T(2,128)(2,1)} %copy.18), calls=%async_computation.3 | async-start | bytes 3145728 | tf_op jit(solution)/shard_map/all_to_all | solution.py:60
  93.0 0.0 copy-done.1
  93.0 0.5 broadcast.37
  93.5 0.8 reduce.3
  94.3 0.1 eq.85
  94.5 22.6 %all-to-all-done.2 = bf16[128,2,3072]{2,1,0:T(2,128)(2,1)S(1)} async-done(((bf16[128,2,3072]{2,1,0:T(2,128)(2,1)}), bf16[128,2,3072]{2,1,0:T(2,128)(2,1)S(1)}, u32[]{:S(2)}, u32[]{:S(2)}) %all-to-all-start.2) | async-done | bytes 1572896 | tf_op jit(solution)/shard_map/all_to_all | solution.py:60
  117.1 0.6 reshape.73
  117.7 0.7 copy.19
  118.4 0.0 copy-start.2
  118.4 0.5 fusion.11
  118.9 0.0 copy-done
  118.9 0.2 fusion.2
  119.1 0.0 copy-done.2
  119.2 0.7 abs_reduce_fusion
  (3 shorter events, 0.0 us)
Async XLA Ops:
  6.5 112.4 %copy-start = (f32[8,6]{1,0:T(8,128)S(1)}, f32[8,6]{1,0:T(8,128)}, u32[]{:S(2)}) copy-start(f32[8,6]{1,0:T(8,128)} %param.14) | copy-start | bytes 580
  6.5 72.5 %reduce-scatter.2.cloned.1.call-start = ((), (), s32[]{:S(2)}) async-start(), calls=%async_computation.4 | async-start | bytes 7077888 | tf_op jit(solution)/shard_map/reduce_scatter | solution.py:38
  40.5 44.0 %all-to-all-start = ((s32[128,1,2]{2,1,0:T(1,128)}), s32[128,1,2]{2,1,0:T(1,128)S(1)}, u32[]{:S(2)}, u32[]{:S(2)}) async-start(s32[128,1,2]{2,1,0:T(1,128)} %bitcast.2), calls=%async_computation | async-start | bytes 131072 | tf_op jit(solution)/shard_map/all_to_all | solution.py:67
  84.5 8.5 %copy-start.1 = (s32[4,8]{1,0:T(4,128)S(1)}, s32[4,8]{1,0:T(4,128)}, u32[]{:S(2)}) copy-start(s32[4,8]{1,0:T(4,128)} %param.13) | copy-start | bytes 388
  84.5 32.6 %all-to-all-start.2 = ((bf16[128,2,3072]{2,1,0:T(2,128)(2,1)}), bf16[128,2,3072]{2,1,0:T(2,128)(2,1)S(1)}, u32[]{:S(2)}, u32[]{:S(2)}) async-start(bf16[128,2,3072]{2,1,0:T(2,128)(2,1)} %copy.18), calls=%async_computation.3 | async-start | bytes 3145728 | tf_op jit(solution)/shard_map/all_to_all | solution.py:60
  118.4 0.7 copy-start.2
Sparse Core Ops, SparseCore 0:
  37.6 41.3 reduce-scatter.1
